TPU v7x, 512 devices: a whole 4x8x8 slice. The times are simulated.
512 devices in a mesh: ctx: 128 (over z_hi, x, y), head: 4 (over z_lo, core).
Axes of the slice: x: 4, y: 8, z: 8 (z_hi: 4, z_lo: 2; z = z_hi * 2 + z_lo), core: 2. Of those that a mesh axis runs over, the one named last changes fastest.
Arguments:
- queries: bfloat16 [32768, 4096], P(('ctx', 'head')), may hold values from -200 to 200
- normed_key_state: bfloat16 [32768, 2048], P(('ctx', 'head')), may hold values from -5 to 5
- value_state_rows: bfloat16 [32768, 2048], P(('ctx', 'head')), may hold values from -6 to 6
- output_gradient: bfloat16 [32768, 4096], P(('ctx', 'head')), may hold values from -6 to 6
- doc_start: int32 [32768], P('ctx'), may hold values from 0 to 32767, as said below
Outputs:
- grad_queries: bfloat16 [32768, 4096], P(('ctx', 'head'))
- key_gradient: bfloat16 [32768, 2048], P(('ctx', 'head'))
- value_gradient: bfloat16 [32768, 2048], P(('ctx', 'head'))
Inputs may be any that keep to these rules, and one draw needn't show every extreme that they name: doc_start[t] is the first position of the document that holds token t: doc_start[0] = 0, each doc_start[t] equals t or doc_start[t - 1], and the last token, position 32767, begins a document of its own.
All inputs are finite; a program needn't handle non-finite values.
Results may differ from a plain program's by a relative error of at most 0.007.
Values may be sent and summed in bfloat16 or wider, within the bound.
No kernel may reach another device: no remote copies, remote signals or barrier semaphores. Data moves between devices by JAX's collectives and lax.ppermute only.
A program may use at most 64 MiB of HBM per device.

v0:
```python
import jax
import jax.numpy as jnp
from jax import lax
from jax.sharding import PartitionSpec as P

QUERY_HEADS = 32
KEY_VALUE_HEADS = 16
HEAD_SIZE = 128
WINDOW = 512
SPAN = 2
CHUNKS = 2
CHAIN = False
score_scale = 168.0 ** (-0.5)


def passed_along(block, axis, distance):
    devices = range(lax.axis_size(axis))
    route = [(i - distance, i) for i in devices if i - distance in devices]
    return lax.ppermute(block, axis, route)


def pair_scores(query_heads, key_block):
    return score_scale * jnp.einsum(
        "tgjd,kgd->gjtk", query_heads, key_block, preferred_element_type=jnp.float32
    )


def attend_chunk(kv_in, qg_in, doc_start):
    kv_all = lax.all_to_all(kv_in, "head", split_axis=1, concat_axis=0, tiled=True)
    tok_rows = kv_all.shape[0]
    kv_cols = kv_all.shape[-1]
    kv_groups = kv_cols // HEAD_SIZE
    group_share = QUERY_HEADS // KEY_VALUE_HEADS
    kv_local = jnp.moveaxis(kv_all[:, 0], 1, 0)
    kv_blocks = [kv_local]
    for distance in range(1, SPAN + 1):
        if CHAIN:
            kv_blocks.append(passed_along(kv_blocks[-1], "ctx", 1))
        else:
            kv_blocks.append(passed_along(kv_local, "ctx", distance))
    qg_all = lax.all_to_all(qg_in, "head", split_axis=1, concat_axis=0, tiled=True)
    query_heads = qg_all[:, 0, 0].reshape(tok_rows, kv_groups, group_share, HEAD_SIZE)
    grad_heads = qg_all[:, 0, 1].reshape(tok_rows, kv_groups, group_share, HEAD_SIZE)
    shard_index = lax.axis_index("ctx")
    local_iota = jnp.arange(tok_rows, dtype=jnp.int32)
    query_pos = shard_index * tok_rows + local_iota

    def visible(distance):
        key_pos = (shard_index - distance) * tok_rows + local_iota
        return (
            (key_pos[None, :] >= doc_start[:, None])
            & (key_pos[None, :] <= query_pos[:, None])
            & (query_pos[:, None] - key_pos[None, :] < WINDOW)
        )

    def unpack(kv_block):
        return (
            kv_block[0].reshape(tok_rows, kv_groups, HEAD_SIZE),
            kv_block[1].reshape(tok_rows, kv_groups, HEAD_SIZE),
        )

    masks = [visible(distance) for distance in range(SPAN + 1)]
    stat_shape = (kv_groups, group_share, tok_rows)
    running = (
        jnp.full(stat_shape, -jnp.inf, jnp.float32),
        jnp.zeros(stat_shape, jnp.float32),
        jnp.zeros(stat_shape, jnp.float32),
    )
    for distance in range(SPAN + 1):
        gather_key_block, gather_value_block = unpack(kv_blocks[distance])
        gather_masked = jnp.where(
            masks[distance], pair_scores(query_heads, gather_key_block), -jnp.inf
        )
        gather_dprob = jnp.einsum(
            "tgjd,kgd->gjtk", grad_heads, gather_value_block, preferred_element_type=jnp.float32
        )
        new_max = jnp.maximum(running[0], jnp.max(gather_masked, axis=-1))
        factor = jnp.exp(running[0] - new_max)
        weights = jnp.exp(gather_masked - new_max[..., None])
        running = (
            new_max,
            running[1] * factor + jnp.sum(weights, axis=-1),
            running[2] * factor + jnp.sum(weights * gather_dprob, axis=-1),
        )
    log_total = running[0] + jnp.log(running[1])
    delta = running[2] / running[1]
    query_total = jnp.zeros((tok_rows, kv_groups, group_share, HEAD_SIZE), jnp.float32)
    kv_parts = {}
    for distance in reversed(range(SPAN + 1)):
        key_block, value_block = unpack(kv_blocks[distance])
        masked = jnp.where(masks[distance], pair_scores(query_heads, key_block), -jnp.inf)
        prob = jnp.exp(masked - log_total[..., None])
        dprob = jnp.einsum(
            "tgjd,kgd->gjtk", grad_heads, value_block, preferred_element_type=jnp.float32
        )
        dscore = (prob * (dprob - delta[..., None])).astype(jnp.bfloat16)
        prob_half = prob.astype(jnp.bfloat16)
        query_part = score_scale * jnp.einsum(
            "gjtk,kgd->tgjd", dscore, key_block, preferred_element_type=jnp.float32
        )
        key_part = score_scale * jnp.einsum(
            "gjtk,tgjd->kgd", dscore, query_heads, preferred_element_type=jnp.float32
        )
        value_part = jnp.einsum(
            "gjtk,tgjd->kgd", prob_half, grad_heads, preferred_element_type=jnp.float32
        )
        query_total = query_total + query_part
        kv_parts[distance] = jnp.stack([key_part, value_part]).reshape(2, tok_rows, kv_cols)
    if CHAIN:
        carried = passed_along(kv_parts[2].astype(jnp.bfloat16), "ctx", -1)
        carried = passed_along((kv_parts[1] + carried).astype(jnp.bfloat16), "ctx", -1)
        kv_total = kv_parts[0] + carried
    else:
        kv_total = kv_parts[0]
        for distance in range(1, SPAN + 1):
            kv_total = kv_total + passed_along(
                kv_parts[distance].astype(jnp.bfloat16), "ctx", -distance
            )
    grad_query_loc = query_total.reshape(tok_rows, 1, kv_groups * group_share * HEAD_SIZE)
    grad_q = lax.all_to_all(
        grad_query_loc.astype(jnp.bfloat16), "head", split_axis=0, concat_axis=1, tiled=True
    )
    kv_out = jnp.moveaxis(kv_total.astype(jnp.bfloat16), 0, 1)[:, None]
    kv_back = lax.all_to_all(kv_out, "head", split_axis=0, concat_axis=1, tiled=True)
    return (grad_q, kv_back)


def local(queries, normed_key_state, value_state_rows, output_gradient, doc_start):
    heads_ax = lax.axis_size("head")
    rows_in = queries.shape[0]
    kv_cols = normed_key_state.shape[1] // (heads_ax * CHUNKS)
    q_cols = queries.shape[1] // (heads_ax * CHUNKS)
    keys = normed_key_state.reshape(rows_in, heads_ax, CHUNKS, kv_cols)
    values = value_state_rows.reshape(rows_in, heads_ax, CHUNKS, kv_cols)
    qs = queries.reshape(rows_in, heads_ax, CHUNKS, q_cols)
    gs = output_gradient.reshape(rows_in, heads_ax, CHUNKS, q_cols)
    dq_parts, dkv_parts = ([], [])
    for chunk in range(CHUNKS):
        kv_in = jnp.stack([keys[:, :, chunk], values[:, :, chunk]], axis=2)
        qg_in = jnp.stack([qs[:, :, chunk], gs[:, :, chunk]], axis=2)
        dq, dkv = attend_chunk(kv_in, qg_in, doc_start)
        dq_parts.append(dq)
        dkv_parts.append(dkv)
    grad_q = jnp.stack(dq_parts, axis=2).reshape(rows_in, heads_ax * CHUNKS * q_cols)
    dkv = jnp.stack(dkv_parts, axis=3)
    grad_k = dkv[:, :, 0].reshape(rows_in, heads_ax * CHUNKS * kv_cols)
    grad_v = dkv[:, :, 1].reshape(rows_in, heads_ax * CHUNKS * kv_cols)
    return (grad_q, grad_k, grad_v)


def solution(mesh):
    placed = (
        P(("ctx", "head"), None),
        P(("ctx", "head"), None),
        P(("ctx", "head"), None),
        P(("ctx", "head"), None),
        P("ctx"),
    )
    return jax.shard_map(
        local,
        mesh=mesh,
        in_specs=placed,
        out_specs=(P(("ctx", "head"), None), P(("ctx", "head"), None), P(("ctx", "head"), None)),
        check_vma=False,
    )
```

profile of v0, /device:TPU:184, one launch (start us, length us, event | category | flops | bytes accessed | tf_op | source)
XLA Modules:
  0.0 210.7 jit_solution(13500736151918691449)
XLA Ops:
  4.3 3.6 %all-to-all-start = ((bf16[64,4,2,256]{3,2,0,1:T(2,128)(2,1)}), bf16[64,4,2,256]{3,2,0,1:T(2,128)(2,1)S(1)}, u32[]{:S(2)}, u32[]{:S(2)}) async-start(bf16[64,4,2,256]{3,2,0,1:T(2,128)(2,1)} %copy.203), calls=%async_computation | async-start | bytes 524288 | tf_op jit(solution)/shard_map/all_to_all | solution.py:29
  17.1 3.4 %all-to-all-start.3 = ((bf16[64,4,2,256]{3,2,0,1:T(2,128)(2,1)}), bf16[64,4,2,256]{3,2,0,1:T(2,128)(2,1)S(1)}, u32[]{:S(2)}, u32[]{:S(2)}) async-start(bf16[64,4,2,256]{3,2,0,1:T(2,128)(2,1)} %copy.231), calls=%async_computation.3 | async-start | bytes 524288 | tf_op jit(solution)/shard_map/all_to_all | solution.py:29
  22.1 3.6 %collective-permute-start = (bf16[2,256,256]{2,1,0:T(8,128)(2,1)S(1)}, bf16[2,256,256]{2,1,0:T(8,128)(2,1)S(1)}, u32[]{:S(2)}, u32[]{:S(2)}) collective-permute-start(bf16[2,256,256]{2,1,0:T(8,128)(2,1)S(1)} %bitcast.375), channel_id=1, source_target_pairs={{0,8},{4,12},{8,16},{12,20},{16,24},{20,28},{24,32},{28,36},{32,40... | collective-permute-start | bytes 786440 | tf_op jit(solution)/shard_map/ppermute | solution.py:19
  25.8 3.5 %collective-permute-start.1 = (bf16[2,256,256]{2,1,0:T(8,128)(2,1)S(1)}, bf16[2,256,256]{2,1,0:T(8,128)(2,1)S(1)}, u32[]{:S(2)}, u32[]{:S(2)}) collective-permute-start(bf16[2,256,256]{2,1,0:T(8,128)(2,1)S(1)} %bitcast.377), channel_id=1, source_target_pairs={{0,4},{4,8},{8,12},{12,16},{16,20},{20,24},{24,28},{28,32},{32,36}... | collective-permute-start | bytes 786440 | tf_op jit(solution)/shard_map/ppermute | solution.py:19
  29.3 3.5 %all-to-all-start.1 = ((bf16[64,4,2,512]{3,2,0,1:T(2,128)(2,1)}), bf16[64,4,2,512]{3,2,0,1:T(2,128)(2,1)S(1)}, u32[]{:S(2)}, u32[]{:S(2)}) async-start(bf16[64,4,2,512]{3,2,0,1:T(2,128)(2,1)} %copy.206), calls=%async_computation.1 | async-start | bytes 1048576 | tf_op jit(solution)/shard_map/all_to_all | solution.py:41
  32.8 3.5 %collective-permute-start.3 = (bf16[2,256,256]{2,1,0:T(8,128)(2,1)S(1)}, bf16[2,256,256]{2,1,0:T(8,128)(2,1)S(1)}, u32[]{:S(2)}, u32[]{:S(2)}) collective-permute-start(bf16[2,256,256]{2,1,0:T(8,128)(2,1)S(1)} %bitcast.373), channel_id=1, source_target_pairs={{0,4},{4,8},{8,12},{12,16},{16,20},{20,24},{24,28},{28,32},{32,36}... | collective-permute-start | bytes 786440 | tf_op jit(solution)/shard_map/ppermute | solution.py:19
  36.3 4.8 %collective-permute-start.2 = (bf16[2,256,256]{2,1,0:T(8,128)(2,1)S(1)}, bf16[2,256,256]{2,1,0:T(8,128)(2,1)S(1)}, u32[]{:S(2)}, u32[]{:S(2)}) collective-permute-start(bf16[2,256,256]{2,1,0:T(8,128)(2,1)S(1)} %bitcast.374), channel_id=1, source_target_pairs={{0,8},{4,12},{8,16},{12,20},{16,24},{20,28},{24,32},{28,36},{32,40... | collective-permute-start | bytes 786440 | tf_op jit(solution)/shard_map/ppermute | solution.py:19
  47.0 3.4 %collective-permute-done.3 = bf16[2,256,256]{2,1,0:T(8,128)(2,1)S(1)} collective-permute-done((bf16[2,256,256]{2,1,0:T(8,128)(2,1)S(1)}, bf16[2,256,256]{2,1,0:T(8,128)(2,1)S(1)}, u32[]{:S(2)}, u32[]{:S(2)}) %collective-permute-start.3) | collective-permute-done | bytes 262176 | tf_op jit(solution)/shard_map/ppermute | solution.py:19
  51.1 10.6 %collective-permute-done.2 = bf16[2,256,256]{2,1,0:T(8,128)(2,1)S(1)} collective-permute-done((bf16[2,256,256]{2,1,0:T(8,128)(2,1)S(1)}, bf16[2,256,256]{2,1,0:T(8,128)(2,1)S(1)}, u32[]{:S(2)}, u32[]{:S(2)}) %collective-permute-start.2) | collective-permute-done | bytes 262176 | tf_op jit(solution)/shard_map/ppermute | solution.py:19
  64.0 3.7 %all-to-all-start.4 = ((bf16[64,4,2,512]{3,2,0,1:T(2,128)(2,1)}), bf16[64,4,2,512]{3,2,0,1:T(2,128)(2,1)S(1)}, u32[]{:S(2)}, u32[]{:S(2)}) async-start(bf16[64,4,2,512]{3,2,0,1:T(2,128)(2,1)} %copy.234), calls=%async_computation.4 | async-start | bytes 1048576 | tf_op jit(solution)/shard_map/all_to_all | solution.py:41
  111.3 6.5 %collective-permute-start.5 = (bf16[2,256,256]{2,0,1:T(2,128)(2,1)}, bf16[2,256,256]{2,0,1:T(2,128)(2,1)}, u32[]{:S(2)}, u32[]{:S(2)}) collective-permute-start(bf16[2,256,256]{2,0,1:T(2,128)(2,1)} %pad_maximum_fusion.7), channel_id=1, source_target_pairs={{8,0},{12,4},{16,8},{20,12},{24,16},{28,20},{32,24},{36,28},{40,32... | collective-permute-start | bytes 786440 | tf_op jit(solution)/shard_map/ppermute | solution.py:19
  122.3 2.1 %collective-permute-start.6 = (bf16[2,256,256]{2,0,1:T(2,128)(2,1)}, bf16[2,256,256]{2,0,1:T(2,128)(2,1)}, u32[]{:S(2)}, u32[]{:S(2)}) collective-permute-start(bf16[2,256,256]{2,0,1:T(2,128)(2,1)} %pad_maximum_fusion.8), channel_id=1, source_target_pairs={{4,0},{8,4},{12,8},{16,12},{20,16},{24,20},{28,24},{32,28},{36,32}... | collective-permute-start | bytes 786440 | tf_op jit(solution)/shard_map/ppermute | solution.py:19
  128.9 2.3 %pad_maximum_fusion.9 = bf16[2,256,256]{2,0,1:T(2,128)(2,1)} fusion(bf16[1,256,256]{2,0,1:T(2,128)(2,1)} %copy.285, bf16[1,256,256]{2,0,1:T(2,128)(2,1)} %copy.284), kind=kLoop, calls=%fused_computation.118 | loop fusion | flops 524288 | bytes 524288 | tf_op jit(solution)/shard_map/stack | solution.py:108
  131.3 25.7 %collective-permute-start.7 = (bf16[2,256,256]{2,0,1:T(2,128)(2,1)}, bf16[2,256,256]{2,0,1:T(2,128)(2,1)}, u32[]{:S(2)}, u32[]{:S(2)}) collective-permute-start(bf16[2,256,256]{2,0,1:T(2,128)(2,1)} %pad_maximum_fusion.9), channel_id=1, source_target_pairs={{8,0},{12,4},{16,8},{20,12},{24,16},{28,20},{32,24},{36,28},{40,32... | collective-permute-start | bytes 786440 | tf_op jit(solution)/shard_map/ppermute | solution.py:19
  161.3 3.6 %all-to-all-start.2 = ((bf16[4,2,16384]{2,1,0:T(2,128)(2,1)}), bf16[4,2,16384]{2,1,0:T(2,128)(2,1)S(1)}, u32[]{:S(2)}, u32[]{:S(2)}) async-start(bf16[4,2,16384]{2,1,0:T(2,128)(2,1)} %reshape.273), calls=%async_computation.2 | async-start | bytes 524288 | tf_op jit(solution)/shard_map/all_to_all | solution.py:120
  168.1 12.0 %all-to-all-done.2 = bf16[4,2,16384]{2,1,0:T(2,128)(2,1)S(1)} async-done(((bf16[4,2,16384]{2,1,0:T(2,128)(2,1)}), bf16[4,2,16384]{2,1,0:T(2,128)(2,1)S(1)}, u32[]{:S(2)}, u32[]{:S(2)}) %all-to-all-start.2) | async-done | bytes 262176 | tf_op jit(solution)/shard_map/all_to_all | solution.py:120
  180.1 3.4 %all-to-all-start.5 = ((bf16[4,2,16384]{2,1,0:T(2,128)(2,1)}), bf16[4,2,16384]{2,1,0:T(2,128)(2,1)S(1)}, u32[]{:S(2)}, u32[]{:S(2)}) async-start(bf16[4,2,16384]{2,1,0:T(2,128)(2,1)} %reshape.271), calls=%async_computation.5 | async-start | bytes 524288 | tf_op jit(solution)/shard_map/all_to_all | solution.py:120
  184.9 2.4 %fusion.67 = bf16[256,1,2,256]{3,2,1,0:T(2,128)(2,1)} fusion(bf16[2,256,256]{2,0,1:T(2,128)(2,1)} %collective-permute-done.5, bf16[2,256,256]{2,0,1:T(2,128)(2,1)} %collective-permute-done.4, f32[1,256,256]{2,0,1:T(1,128)S(1)} %copy-done.26, f32[1,256,256]{2,0,1:T(1,128)S(1)} %copy-done.27), kind=kLoop, calls=%fused_computation.128 | loop fusion | flops 786432 | bytes 1310720 | tf_op jit(solution)/shard_map/broadcast_in_dim | solution.py:123
  187.3 2.2 %all-to-all-done.5 = bf16[4,2,16384]{2,1,0:T(2,128)(2,1)S(1)} async-done(((bf16[4,2,16384]{2,1,0:T(2,128)(2,1)}), bf16[4,2,16384]{2,1,0:T(2,128)(2,1)S(1)}, u32[]{:S(2)}, u32[]{:S(2)}) %all-to-all-start.5) | async-done | bytes 262176 | tf_op jit(solution)/shard_map/all_to_all | solution.py:120
  189.5 3.4 %all-to-all-start.6 = ((bf16[256,1,2,256]{3,2,1,0:T(2,128)(2,1)}), bf16[256,1,2,256]{3,2,1,0:T(2,128)(2,1)S(1)}, u32[]{:S(2)}, u32[]{:S(2)}) async-start(bf16[256,1,2,256]{3,2,1,0:T(2,128)(2,1)} %fusion.67), calls=%async_computation.6 | async-start | bytes 524288 | tf_op jit(solution)/shard_map/all_to_all | solution.py:124
  193.4 2.4 %fusion.66 = bf16[256,1,2,256]{3,2,1,0:T(2,128)(2,1)} fusion(bf16[2,256,256]{2,0,1:T(2,128)(2,1)} %collective-permute-done.7, bf16[2,256,256]{2,0,1:T(2,128)(2,1)} %collective-permute-done.6, f32[1,256,256]{2,0,1:T(1,128)S(1)} %copy.277, f32[1,256,256]{2,0,1:T(1,128)S(1)} %copy.276), kind=kLoop, calls=%fused_computation.127 | loop fusion | flops 786432 | bytes 1310720 | tf_op jit(solution)/shard_map/broadcast_in_dim | solution.py:123
  195.8 3.1 %all-to-all-done.6 = bf16[256,1,2,256]{3,2,1,0:T(2,128)(2,1)S(1)} async-done(((bf16[256,1,2,256]{3,2,1,0:T(2,128)(2,1)}), bf16[256,1,2,256]{3,2,1,0:T(2,128)(2,1)S(1)}, u32[]{:S(2)}, u32[]{:S(2)}) %all-to-all-start.6) | async-done | bytes 262176 | tf_op jit(solution)/shard_map/all_to_all | solution.py:124
  198.9 3.4 %all-to-all-start.7 = ((bf16[256,1,2,256]{3,2,1,0:T(2,128)(2,1)}), bf16[256,1,2,256]{3,2,1,0:T(2,128)(2,1)S(1)}, u32[]{:S(2)}, u32[]{:S(2)}) async-start(bf16[256,1,2,256]{3,2,1,0:T(2,128)(2,1)} %fusion.66), calls=%async_computation.7 | async-start | bytes 524288 | tf_op jit(solution)/shard_map/all_to_all | solution.py:124
  204.8 3.4 %all-to-all-done.7 = bf16[256,1,2,256]{3,2,1,0:T(2,128)(2,1)S(1)} async-done(((bf16[256,1,2,256]{3,2,1,0:T(2,128)(2,1)}), bf16[256,1,2,256]{3,2,1,0:T(2,128)(2,1)S(1)}, u32[]{:S(2)}, u32[]{:S(2)}) %all-to-all-start.7) | async-done | bytes 262176 | tf_op jit(solution)/shard_map/all_to_all | solution.py:124
  (240 shorter events, 89.4 us)
Async XLA Ops:
  4.3 12.8 %all-to-all-start = ((bf16[64,4,2,256]{3,2,0,1:T(2,128)(2,1)}), bf16[64,4,2,256]{3,2,0,1:T(2,128)(2,1)S(1)}, u32[]{:S(2)}, u32[]{:S(2)}) async-start(bf16[64,4,2,256]{3,2,0,1:T(2,128)(2,1)} %copy.203), calls=%async_computation | async-start | bytes 524288 | tf_op jit(solution)/shard_map/all_to_all | solution.py:29
  17.1 12.2 %all-to-all-start.3 = ((bf16[64,4,2,256]{3,2,0,1:T(2,128)(2,1)}), bf16[64,4,2,256]{3,2,0,1:T(2,128)(2,1)S(1)}, u32[]{:S(2)}, u32[]{:S(2)}) async-start(bf16[64,4,2,256]{3,2,0,1:T(2,128)(2,1)} %copy.231), calls=%async_computation.3 | async-start | bytes 524288 | tf_op jit(solution)/shard_map/all_to_all | solution.py:29
  22.1 46.0 %copy-start.33 = (pred[256,256]{0,1:T(8,128)(4,1)}, pred[256,256]{0,1:T(8,128)(4,1)S(1)}, u32[]{:S(2)}) copy-start(pred[256,256]{0,1:T(8,128)(4,1)S(1)} %get-tuple-element.57) | copy-start | bytes 196612
  22.1 20.8 %collective-permute-start = (bf16[2,256,256]{2,1,0:T(8,128)(2,1)S(1)}, bf16[2,256,256]{2,1,0:T(8,128)(2,1)S(1)}, u32[]{:S(2)}, u32[]{:S(2)}) collective-permute-start(bf16[2,256,256]{2,1,0:T(8,128)(2,1)S(1)} %bitcast.375), channel_id=1, source_target_pairs={{0,8},{4,12},{8,16},{12,20},{16,24},{20,28},{24,32},{28,36},{32,40... | collective-permute-start | bytes 786440 | tf_op jit(solution)/shard_map/ppermute | solution.py:19
  25.8 18.8 %collective-permute-start.1 = (bf16[2,256,256]{2,1,0:T(8,128)(2,1)S(1)}, bf16[2,256,256]{2,1,0:T(8,128)(2,1)S(1)}, u32[]{:S(2)}, u32[]{:S(2)}) collective-permute-start(bf16[2,256,256]{2,1,0:T(8,128)(2,1)S(1)} %bitcast.377), channel_id=1, source_target_pairs={{0,4},{4,8},{8,12},{12,16},{16,20},{20,24},{24,28},{28,32},{32,36}... | collective-permute-start | bytes 786440 | tf_op jit(solution)/shard_map/ppermute | solution.py:19
  29.3 34.8 %all-to-all-start.1 = ((bf16[64,4,2,512]{3,2,0,1:T(2,128)(2,1)}), bf16[64,4,2,512]{3,2,0,1:T(2,128)(2,1)S(1)}, u32[]{:S(2)}, u32[]{:S(2)}) async-start(bf16[64,4,2,512]{3,2,0,1:T(2,128)(2,1)} %copy.206), calls=%async_computation.1 | async-start | bytes 1048576 | tf_op jit(solution)/shard_map/all_to_all | solution.py:41
  32.8 17.5 %collective-permute-start.3 = (bf16[2,256,256]{2,1,0:T(8,128)(2,1)S(1)}, bf16[2,256,256]{2,1,0:T(8,128)(2,1)S(1)}, u32[]{:S(2)}, u32[]{:S(2)}) collective-permute-start(bf16[2,256,256]{2,1,0:T(8,128)(2,1)S(1)} %bitcast.373), channel_id=1, source_target_pairs={{0,4},{4,8},{8,12},{12,16},{16,20},{20,24},{24,28},{28,32},{32,36}... | collective-permute-start | bytes 786440 | tf_op jit(solution)/shard_map/ppermute | solution.py:19
  36.3 25.4 %collective-permute-start.2 = (bf16[2,256,256]{2,1,0:T(8,128)(2,1)S(1)}, bf16[2,256,256]{2,1,0:T(8,128)(2,1)S(1)}, u32[]{:S(2)}, u32[]{:S(2)}) collective-permute-start(bf16[2,256,256]{2,1,0:T(8,128)(2,1)S(1)} %bitcast.374), channel_id=1, source_target_pairs={{0,8},{4,12},{8,16},{12,20},{16,24},{20,28},{24,32},{28,36},{32,40... | collective-permute-start | bytes 786440 | tf_op jit(solution)/shard_map/ppermute | solution.py:19
  41.3 26.9 %copy-start.16 = (bf16[1,256,256]{1,2,0:T(8,128)(2,1)}, bf16[1,256,256]{1,2,0:T(8,128)(2,1)S(1)}, u32[]{:S(2)}) copy-start(bf16[1,256,256]{1,2,0:T(8,128)(2,1)S(1)} %copy.211) | copy-start | bytes 393220
  45.4 24.0 %copy-start.20 = (bf16[1,256,256]{1,2,0:T(8,128)(2,1)}, bf16[1,256,256]{1,2,0:T(8,128)(2,1)S(1)}, u32[]{:S(2)}) copy-start(bf16[1,256,256]{1,2,0:T(8,128)(2,1)S(1)} %copy.214) | copy-start | bytes 393220
  64.0 16.1 %all-to-all-start.4 = ((bf16[64,4,2,512]{3,2,0,1:T(2,128)(2,1)}), bf16[64,4,2,512]{3,2,0,1:T(2,128)(2,1)S(1)}, u32[]{:S(2)}, u32[]{:S(2)}) async-start(bf16[64,4,2,512]{3,2,0,1:T(2,128)(2,1)} %copy.234), calls=%async_computation.4 | async-start | bytes 1048576 | tf_op jit(solution)/shard_map/all_to_all | solution.py:41
  70.2 6.9 %copy-start = (f32[2,2,256,256]{2,3,1,0:T(8,128)}, f32[2,2,256,256]{2,3,1,0:T(8,128)S(1)}, u32[]{:S(2)}) copy-start(f32[2,2,256,256]{2,3,1,0:T(8,128)S(1)} %get-tuple-element.72) | copy-start | bytes 3145732
  104.8 79.2 %collective-permute-start.4 = (bf16[2,256,256]{2,0,1:T(2,128)(2,1)}, bf16[2,256,256]{2,0,1:T(2,128)(2,1)}, u32[]{:S(2)}, u32[]{:S(2)}) collective-permute-start(bf16[2,256,256]{2,0,1:T(2,128)(2,1)} %pad_maximum_fusion.6), channel_id=1, source_target_pairs={{4,0},{8,4},{12,8},{16,12},{20,16},{24,20},{28,24},{32,28},{36,32}... | collective-permute-start | bytes 786440 | tf_op jit(solution)/shard_map/ppermute | solution.py:19
  111.3 72.7 %collective-permute-start.5 = (bf16[2,256,256]{2,0,1:T(2,128)(2,1)}, bf16[2,256,256]{2,0,1:T(2,128)(2,1)}, u32[]{:S(2)}, u32[]{:S(2)}) collective-permute-start(bf16[2,256,256]{2,0,1:T(2,128)(2,1)} %pad_maximum_fusion.7), channel_id=1, source_target_pairs={{8,0},{12,4},{16,8},{20,12},{24,16},{28,20},{32,24},{36,28},{40,32... | collective-permute-start | bytes 786440 | tf_op jit(solution)/shard_map/ppermute | solution.py:19
  122.3 71.2 %collective-permute-start.6 = (bf16[2,256,256]{2,0,1:T(2,128)(2,1)}, bf16[2,256,256]{2,0,1:T(2,128)(2,1)}, u32[]{:S(2)}, u32[]{:S(2)}) collective-permute-start(bf16[2,256,256]{2,0,1:T(2,128)(2,1)} %pad_maximum_fusion.8), channel_id=1, source_target_pairs={{4,0},{8,4},{12,8},{16,12},{20,16},{24,20},{28,24},{32,28},{36,32}... | collective-permute-start | bytes 786440 | tf_op jit(solution)/shard_map/ppermute | solution.py:19
  127.1 29.9 %copy-start.14 = (f32[2,128,2,256]{3,1,2,0:T(8,128)S(1)}, f32[2,128,2,256]{3,1,2,0:T(8,128)}, u32[]{:S(2)}) copy-start(f32[2,128,2,256]{3,1,2,0:T(8,128)} %fusion.89) | copy-start | bytes 1572868
  128.9 28.1 %copy-start.13 = (f32[2,128,2,256]{3,1,2,0:T(8,128)S(1)}, f32[2,128,2,256]{3,1,2,0:T(8,128)}, u32[]{:S(2)}) copy-start(f32[2,128,2,256]{3,1,2,0:T(8,128)} %fusion.88) | copy-start | bytes 1572868
  128.9 28.1 %copy-start.23 = (bf16[1,256,256]{1,2,0:T(8,128)(2,1)S(1)}, bf16[1,256,256]{1,2,0:T(8,128)(2,1)}, u32[]{:S(2)}) copy-start(bf16[1,256,256]{1,2,0:T(8,128)(2,1)} %copy.205) | copy-start | bytes 393220
  131.3 62.1 %collective-permute-start.7 = (bf16[2,256,256]{2,0,1:T(2,128)(2,1)}, bf16[2,256,256]{2,0,1:T(2,128)(2,1)}, u32[]{:S(2)}, u32[]{:S(2)}) collective-permute-start(bf16[2,256,256]{2,0,1:T(2,128)(2,1)} %pad_maximum_fusion.9), channel_id=1, source_target_pairs={{8,0},{12,4},{16,8},{20,12},{24,16},{28,20},{32,24},{36,28},{40,32... | collective-permute-start | bytes 786440 | tf_op jit(solution)/shard_map/ppermute | solution.py:19
  161.3 18.8 %all-to-all-start.2 = ((bf16[4,2,16384]{2,1,0:T(2,128)(2,1)}), bf16[4,2,16384]{2,1,0:T(2,128)(2,1)S(1)}, u32[]{:S(2)}, u32[]{:S(2)}) async-start(bf16[4,2,16384]{2,1,0:T(2,128)(2,1)} %reshape.273), calls=%async_computation.2 | async-start | bytes 524288 | tf_op jit(solution)/shard_map/all_to_all | solution.py:120
  168.1 15.4 %copy-start.5 = (bf16[256,1,1,512]{0,3,2,1:T(8,128)(2,1)S(1)}, bf16[256,1,1,512]{0,3,2,1:T(8,128)(2,1)}, u32[]{:S(2)}) copy-start(bf16[256,1,1,512]{0,3,2,1:T(8,128)(2,1)} %copy.246) | copy-start | bytes 786436
  180.1 9.4 %all-to-all-start.5 = ((bf16[4,2,16384]{2,1,0:T(2,128)(2,1)}), bf16[4,2,16384]{2,1,0:T(2,128)(2,1)S(1)}, u32[]{:S(2)}, u32[]{:S(2)}) async-start(bf16[4,2,16384]{2,1,0:T(2,128)(2,1)} %reshape.271), calls=%async_computation.5 | async-start | bytes 524288 | tf_op jit(solution)/shard_map/all_to_all | solution.py:120
  189.5 9.4 %all-to-all-start.6 = ((bf16[256,1,2,256]{3,2,1,0:T(2,128)(2,1)}), bf16[256,1,2,256]{3,2,1,0:T(2,128)(2,1)S(1)}, u32[]{:S(2)}, u32[]{:S(2)}) async-start(bf16[256,1,2,256]{3,2,1,0:T(2,128)(2,1)} %fusion.67), calls=%async_computation.6 | async-start | bytes 524288 | tf_op jit(solution)/shard_map/all_to_all | solution.py:124
  198.9 9.4 %all-to-all-start.7 = ((bf16[256,1,2,256]{3,2,1,0:T(2,128)(2,1)}), bf16[256,1,2,256]{3,2,1,0:T(2,128)(2,1)S(1)}, u32[]{:S(2)}, u32[]{:S(2)}) async-start(bf16[256,1,2,256]{3,2,1,0:T(2,128)(2,1)} %fusion.66), calls=%async_computation.7 | async-start | bytes 524288 | tf_op jit(solution)/shard_map/all_to_all | solution.py:124
  (46 other events, 78.1 us)
where the time goes:
time: 212 us; the launch traced here: 211 us
  starting transfers between devices  79.9 us (38%)
  local copies, waits for them, and re-layouts  43.9 us (21%)
  waiting for transfers between devices  36.4 us (17%)
  matrix products  27.9 us (13%)
  other arithmetic  21 us (10%)
    ppermute x8, starting transfers between devices, passed_along(): return lax.ppermute(block, axis, route)  51.8 us
    ppermute x8, waiting for transfers between devices, passed_along(): return lax.ppermute(block, axis, route)  15.7 us
    all_to_all x2, waiting for transfers between devices, attend_chunk(): lax.all_to_all(grad_query_loc.astype(jnp.bfloat16), 'head', split_axis=0,...  14.2 us
    another operation x12, local copies, waits for them, and re-layouts, attend_chunk(): jnp.stack([key_part, value_part]).reshape(2, tok_rows, kv_cols)  10.3 us
    unnamed x116, local copies, waits for them, and re-layouts  10.1 us
    all_to_all x2, starting transfers between devices, attend_chunk(): lax.all_to_all(qg_in, 'head', split_axis=1, concat_axis=0, tiled=True)  7.13 us
    all_to_all x2, starting transfers between devices, attend_chunk(): lax.all_to_all(kv_in, 'head', split_axis=1, concat_axis=0, tiled=True)  7.07 us
    all_to_all x2, starting transfers between devices, attend_chunk(): lax.all_to_all(grad_query_loc.astype(jnp.bfloat16), 'head', split_axis=0,...  7.05 us
  transfers between devices with their start and end apart: 16, of which 7 were waited for; matrix products, arithmetic and copies ran while one was open for 27% of the time, Pallas kernels for 0%

commit v1 on v0

--- a/solution.py
+++ b/solution.py
@@ -117,8 +117,14 @@
                 kv_parts[distance].astype(jnp.bfloat16), "ctx", -distance
             )
     grad_query_loc = query_total.reshape(tok_rows, 1, kv_groups * group_share * HEAD_SIZE)
-    grad_q = lax.all_to_all(
-        grad_query_loc.astype(jnp.bfloat16), "head", split_axis=0, concat_axis=1, tiled=True
+    grad_q = jnp.concatenate(
+        lax.all_to_all(
+            jnp.stack(jnp.split(grad_query_loc.astype(jnp.bfloat16), lax.axis_size("head"), 0)),
+            axis_name="head",
+            split_axis=0,
+            concat_axis=0,
+        ),
+        1,
     )
     kv_out = jnp.moveaxis(kv_total.astype(jnp.bfloat16), 0, 1)[:, None]
     kv_back = lax.all_to_all(kv_out, "head", split_axis=0, concat_axis=1, tiled=True)

time: 212 us -> 216 us (1.019)
  local copies, waits for them, and re-layouts: 43.9 us -> 47 us
    another operation x12, local copies, waits for them, and re-layouts: 10.3 us -> 16.2 us  [attend_chunk(): jnp.stack([key_part, value_part]).reshape(2, tok_rows, kv_cols)]
    unnamed x116 -> x104, local copies, waits for them, and re-layouts: 10.1 us -> 6.85 us
    another operation x4, other arithmetic: 6.26 us -> 9.2 us  [attend_chunk(): jnp.stack([key_part, value_part]).reshape(2, tok_rows, kv_cols)]
    convert_element_type x2 -> x0, other arithmetic: 2.55 us -> none  [attend_chunk(): grad_query_loc.astype(jnp.bfloat16)]
  transfers between devices with their start and end apart: 16 -> 16, of which waited for: 7 -> 7; matrix products, arithmetic and copies ran while one was open for 27% -> 28% of each run, Pallas kernels for 0% -> 0%
where the time goes in v1:
time: 216 us; the launch traced here: 215 us
  starting transfers between devices  79.8 us (37%)
  local copies, waits for them, and re-layouts  47 us (22%)
  waiting for transfers between devices  36.6 us (17%)
  matrix products  27 us (12%)
  other arithmetic  22.8 us (11%)
    ppermute x8, starting transfers between devices, passed_along(): return lax.ppermute(block, axis, route)  51.7 us
    another operation x12, local copies, waits for them, and re-layouts, attend_chunk(): jnp.stack([key_part, value_part]).reshape(2, tok_rows, kv_cols)  16.2 us
    ppermute x8, waiting for transfers between devices, passed_along(): return lax.ppermute(block, axis, route)  15.7 us
    all_to_all x2, waiting for transfers between devices, attend_chunk(): lax.all_to_all(jnp.stack(jnp.split(grad_query_loc.astype(jnp.bfloat16), l...  13.7 us
    another operation x4, other arithmetic, attend_chunk(): jnp.stack([key_part, value_part]).reshape(2, tok_rows, kv_cols)  9.2 us
    all_to_all x2, waiting for transfers between devices, attend_chunk(): lax.all_to_all(kv_out, 'head', split_axis=0, concat_axis=1, tiled=True)  7.18 us
    all_to_all x2, starting transfers between devices, attend_chunk(): lax.all_to_all(qg_in, 'head', split_axis=1, concat_axis=0, tiled=True)  7.13 us
    all_to_all x2, starting transfers between devices, attend_chunk(): lax.all_to_all(kv_in, 'head', split_axis=1, concat_axis=0, tiled=True)  7.07 us
  transfers between devices with their start and end apart: 16, of which 7 were waited for; matrix products, arithmetic and copies ran while one was open for 28% of the time, Pallas kernels for 0%

profile of v1, /device:TPU:184, one launch (start us, length us, event | category | flops | bytes accessed | tf_op | source)
XLA Modules:
  0.0 214.7 jit_solution(13384049019158558989)
XLA Ops:
  4.3 3.6 %all-to-all-start = ((bf16[64,4,2,256]{3,2,0,1:T(2,128)(2,1)}), bf16[64,4,2,256]{3,2,0,1:T(2,128)(2,1)S(1)}, u32[]{:S(2)}, u32[]{:S(2)}) async-start(bf16[64,4,2,256]{3,2,0,1:T(2,128)(2,1)} %copy.291), calls=%async_computation | async-start | bytes 524288 | tf_op jit(solution)/shard_map/all_to_all | solution.py:29
  17.1 3.4 %all-to-all-start.3 = ((bf16[64,4,2,256]{3,2,0,1:T(2,128)(2,1)}), bf16[64,4,2,256]{3,2,0,1:T(2,128)(2,1)S(1)}, u32[]{:S(2)}, u32[]{:S(2)}) async-start(bf16[64,4,2,256]{3,2,0,1:T(2,128)(2,1)} %copy.322), calls=%async_computation.3 | async-start | bytes 524288 | tf_op jit(solution)/shard_map/all_to_all | solution.py:29
  22.1 3.6 %collective-permute-start = (bf16[2,256,256]{2,1,0:T(8,128)(2,1)S(1)}, bf16[2,256,256]{2,1,0:T(8,128)(2,1)S(1)}, u32[]{:S(2)}, u32[]{:S(2)}) collective-permute-start(bf16[2,256,256]{2,1,0:T(8,128)(2,1)S(1)} %bitcast.375), channel_id=1, source_target_pairs={{0,8},{4,12},{8,16},{12,20},{16,24},{20,28},{24,32},{28,36},{32,40... | collective-permute-start | bytes 786440 | tf_op jit(solution)/shard_map/ppermute | solution.py:19
  25.8 3.5 %collective-permute-start.1 = (bf16[2,256,256]{2,1,0:T(8,128)(2,1)S(1)}, bf16[2,256,256]{2,1,0:T(8,128)(2,1)S(1)}, u32[]{:S(2)}, u32[]{:S(2)}) collective-permute-start(bf16[2,256,256]{2,1,0:T(8,128)(2,1)S(1)} %bitcast.377), channel_id=1, source_target_pairs={{0,4},{4,8},{8,12},{12,16},{16,20},{20,24},{24,28},{28,32},{32,36}... | collective-permute-start | bytes 786440 | tf_op jit(solution)/shard_map/ppermute | solution.py:19
  29.3 3.5 %all-to-all-start.1 = ((bf16[64,4,2,512]{3,2,0,1:T(2,128)(2,1)}), bf16[64,4,2,512]{3,2,0,1:T(2,128)(2,1)S(1)}, u32[]{:S(2)}, u32[]{:S(2)}) async-start(bf16[64,4,2,512]{3,2,0,1:T(2,128)(2,1)} %copy.294), calls=%async_computation.1 | async-start | bytes 1048576 | tf_op jit(solution)/shard_map/all_to_all | solution.py:41
  32.8 3.5 %collective-permute-start.3 = (bf16[2,256,256]{2,1,0:T(8,128)(2,1)S(1)}, bf16[2,256,256]{2,1,0:T(8,128)(2,1)S(1)}, u32[]{:S(2)}, u32[]{:S(2)}) collective-permute-start(bf16[2,256,256]{2,1,0:T(8,128)(2,1)S(1)} %bitcast.373), channel_id=1, source_target_pairs={{0,4},{4,8},{8,12},{12,16},{16,20},{20,24},{24,28},{28,32},{32,36}... | collective-permute-start | bytes 786440 | tf_op jit(solution)/shard_map/ppermute | solution.py:19
  36.3 4.8 %collective-permute-start.2 = (bf16[2,256,256]{2,1,0:T(8,128)(2,1)S(1)}, bf16[2,256,256]{2,1,0:T(8,128)(2,1)S(1)}, u32[]{:S(2)}, u32[]{:S(2)}) collective-permute-start(bf16[2,256,256]{2,1,0:T(8,128)(2,1)S(1)} %bitcast.374), channel_id=1, source_target_pairs={{0,8},{4,12},{8,16},{12,20},{16,24},{20,28},{24,32},{28,36},{32,40... | collective-permute-start | bytes 786440 | tf_op jit(solution)/shard_map/ppermute | solution.py:19
  47.0 3.4 %collective-permute-done.3 = bf16[2,256,256]{2,1,0:T(8,128)(2,1)S(1)} collective-permute-done((bf16[2,256,256]{2,1,0:T(8,128)(2,1)S(1)}, bf16[2,256,256]{2,1,0:T(8,128)(2,1)S(1)}, u32[]{:S(2)}, u32[]{:S(2)}) %collective-permute-start.3) | collective-permute-done | bytes 262176 | tf_op jit(solution)/shard_map/ppermute | solution.py:19
  51.1 10.6 %collective-permute-done.2 = bf16[2,256,256]{2,1,0:T(8,128)(2,1)S(1)} collective-permute-done((bf16[2,256,256]{2,1,0:T(8,128)(2,1)S(1)}, bf16[2,256,256]{2,1,0:T(8,128)(2,1)S(1)}, u32[]{:S(2)}, u32[]{:S(2)}) %collective-permute-start.2) | collective-permute-done | bytes 262176 | tf_op jit(solution)/shard_map/ppermute | solution.py:19
  64.0 3.7 %all-to-all-start.4 = ((bf16[64,4,2,512]{3,2,0,1:T(2,128)(2,1)}), bf16[64,4,2,512]{3,2,0,1:T(2,128)(2,1)S(1)}, u32[]{:S(2)}, u32[]{:S(2)}) async-start(bf16[64,4,2,512]{3,2,0,1:T(2,128)(2,1)} %copy.325), calls=%async_computation.4 | async-start | bytes 1048576 | tf_op jit(solution)/shard_map/all_to_all | solution.py:41
  105.0 2.3 %pad_maximum_fusion.8 = bf16[2,256,256]{2,0,1:T(2,128)(2,1)} fusion(bf16[1,256,256]{2,0,1:T(2,128)(2,1)} %copy.361, bf16[1,256,256]{2,0,1:T(2,128)(2,1)} %copy.360), kind=kLoop, calls=%fused_computation.119 | loop fusion | flops 524288 | bytes 524288 | tf_op jit(solution)/shard_map/stack | solution.py:108
  116.0 6.5 %collective-permute-start.5 = (bf16[2,256,256]{2,0,1:T(2,128)(2,1)}, bf16[2,256,256]{2,0,1:T(2,128)(2,1)}, u32[]{:S(2)}, u32[]{:S(2)}) collective-permute-start(bf16[2,256,256]{2,0,1:T(2,128)(2,1)} %pad_maximum_fusion.9), channel_id=1, source_target_pairs={{8,0},{12,4},{16,8},{20,12},{24,16},{28,20},{32,24},{36,28},{40,32... | collective-permute-start | bytes 786440 | tf_op jit(solution)/shard_map/ppermute | solution.py:19
  127.8 2.3 %pad_maximum_fusion.10 = bf16[2,256,256]{2,0,1:T(2,128)(2,1)} fusion(bf16[1,256,256]{2,0,1:T(2,128)(2,1)} %copy.375, bf16[1,256,256]{2,0,1:T(2,128)(2,1)} %copy.374), kind=kLoop, calls=%fused_computation.121 | loop fusion | flops 524288 | bytes 524288 | tf_op jit(solution)/shard_map/stack | solution.py:108
  136.5 2.3 %pad_maximum_fusion.11 = bf16[2,256,256]{2,0,1:T(2,128)(2,1)} fusion(bf16[1,256,256]{2,0,1:T(2,128)(2,1)} %copy.379, bf16[1,256,256]{2,0,1:T(2,128)(2,1)} %copy.378), kind=kLoop, calls=%fused_computation.122 | loop fusion | flops 524288 | bytes 524288 | tf_op jit(solution)/shard_map/stack | solution.py:108
  138.9 26.0 %collective-permute-start.7 = (bf16[2,256,256]{2,0,1:T(2,128)(2,1)}, bf16[2,256,256]{2,0,1:T(2,128)(2,1)}, u32[]{:S(2)}, u32[]{:S(2)}) collective-permute-start(bf16[2,256,256]{2,0,1:T(2,128)(2,1)} %pad_maximum_fusion.11), channel_id=1, source_target_pairs={{8,0},{12,4},{16,8},{20,12},{24,16},{28,20},{32,24},{36,28},{40,32... | collective-permute-start | bytes 786440 | tf_op jit(solution)/shard_map/ppermute | solution.py:19
  166.4 3.7 %all-to-all-start.2 = ((bf16[4,64,1,512]{3,1,2,0:T(8,128)(2,1)}), bf16[4,64,1,512]{3,1,2,0:T(8,128)(2,1)S(1)}, u32[]{:S(2)}, u32[]{:S(2)}) async-start(bf16[4,64,1,512]{3,1,2,0:T(8,128)(2,1)} %pad_maximum_fusion.5), calls=%async_computation.2 | async-start | bytes 524288 | tf_op jit(solution)/shard_map/all_to_all | solution.py:121
  172.6 11.5 %all-to-all-done.2 = bf16[4,64,1,512]{3,1,2,0:T(8,128)(2,1)S(1)} async-done(((bf16[4,64,1,512]{3,1,2,0:T(8,128)(2,1)}), bf16[4,64,1,512]{3,1,2,0:T(8,128)(2,1)S(1)}, u32[]{:S(2)}, u32[]{:S(2)}) %all-to-all-start.2) | async-done | bytes 262176 | tf_op jit(solution)/shard_map/all_to_all | solution.py:121
  184.1 3.4 %all-to-all-start.5 = ((bf16[4,64,1,512]{3,1,2,0:T(8,128)(2,1)}), bf16[4,64,1,512]{3,1,2,0:T(8,128)(2,1)S(1)}, u32[]{:S(2)}, u32[]{:S(2)}) async-start(bf16[4,64,1,512]{3,1,2,0:T(8,128)(2,1)} %pad_maximum_fusion.7), calls=%async_computation.5 | async-start | bytes 524288 | tf_op jit(solution)/shard_map/all_to_all | solution.py:121
  188.9 2.4 %fusion.69 = bf16[256,1,2,256]{3,2,1,0:T(2,128)(2,1)} fusion(bf16[2,256,256]{2,0,1:T(2,128)(2,1)} %collective-permute-done.5, bf16[2,256,256]{2,0,1:T(2,128)(2,1)} %collective-permute-done.4, f32[1,256,256]{2,0,1:T(1,128)S(1)} %copy-done.25, f32[1,256,256]{2,0,1:T(1,128)S(1)} %copy-done.26), kind=kLoop, calls=%fused_computation.132 | loop fusion | flops 786432 | bytes 1310720 | tf_op jit(solution)/shard_map/broadcast_in_dim | solution.py:129
  193.5 3.4 %all-to-all-start.6 = ((bf16[256,1,2,256]{3,2,1,0:T(2,128)(2,1)}), bf16[256,1,2,256]{3,2,1,0:T(2,128)(2,1)S(1)}, u32[]{:S(2)}, u32[]{:S(2)}) async-start(bf16[256,1,2,256]{3,2,1,0:T(2,128)(2,1)} %fusion.69), calls=%async_computation.6 | async-start | bytes 524288 | tf_op jit(solution)/shard_map/all_to_all | solution.py:130
  197.4 2.4 %fusion.68 = bf16[256,1,2,256]{3,2,1,0:T(2,128)(2,1)} fusion(bf16[2,256,256]{2,0,1:T(2,128)(2,1)} %collective-permute-done.7, bf16[2,256,256]{2,0,1:T(2,128)(2,1)} %collective-permute-done.6, f32[1,256,256]{2,0,1:T(1,128)S(1)} %copy.371, f32[1,256,256]{2,0,1:T(1,128)S(1)} %copy.370), kind=kLoop, calls=%fused_computation.131 | loop fusion | flops 786432 | bytes 1310720 | tf_op jit(solution)/shard_map/broadcast_in_dim | solution.py:129
  199.9 3.1 %all-to-all-done.6 = bf16[256,1,2,256]{3,2,1,0:T(2,128)(2,1)S(1)} async-done(((bf16[256,1,2,256]{3,2,1,0:T(2,128)(2,1)}), bf16[256,1,2,256]{3,2,1,0:T(2,128)(2,1)S(1)}, u32[]{:S(2)}, u32[]{:S(2)}) %all-to-all-start.6) | async-done | bytes 262176 | tf_op jit(solution)/shard_map/all_to_all | solution.py:130
  202.9 3.4 %all-to-all-start.7 = ((bf16[256,1,2,256]{3,2,1,0:T(2,128)(2,1)}), bf16[256,1,2,256]{3,2,1,0:T(2,128)(2,1)S(1)}, u32[]{:S(2)}, u32[]{:S(2)}) async-start(bf16[256,1,2,256]{3,2,1,0:T(2,128)(2,1)} %fusion.68), calls=%async_computation.7 | async-start | bytes 524288 | tf_op jit(solution)/shard_map/all_to_all | solution.py:130
  208.2 4.1 %all-to-all-done.7 = bf16[256,1,2,256]{3,2,1,0:T(2,128)(2,1)S(1)} async-done(((bf16[256,1,2,256]{3,2,1,0:T(2,128)(2,1)}), bf16[256,1,2,256]{3,2,1,0:T(2,128)(2,1)S(1)}, u32[]{:S(2)}, u32[]{:S(2)}) %all-to-all-start.7) | async-done | bytes 262176 | tf_op jit(solution)/shard_map/all_to_all | solution.py:130
  (237 shorter events, 92.7 us)
Async XLA Ops:
  4.3 12.8 %all-to-all-start = ((bf16[64,4,2,256]{3,2,0,1:T(2,128)(2,1)}), bf16[64,4,2,256]{3,2,0,1:T(2,128)(2,1)S(1)}, u32[]{:S(2)}, u32[]{:S(2)}) async-start(bf16[64,4,2,256]{3,2,0,1:T(2,128)(2,1)} %copy.291), calls=%async_computation | async-start | bytes 524288 | tf_op jit(solution)/shard_map/all_to_all | solution.py:29
  17.1 12.2 %all-to-all-start.3 = ((bf16[64,4,2,256]{3,2,0,1:T(2,128)(2,1)}), bf16[64,4,2,256]{3,2,0,1:T(2,128)(2,1)S(1)}, u32[]{:S(2)}, u32[]{:S(2)}) async-start(bf16[64,4,2,256]{3,2,0,1:T(2,128)(2,1)} %copy.322), calls=%async_computation.3 | async-start | bytes 524288 | tf_op jit(solution)/shard_map/all_to_all | solution.py:29
  22.1 46.0 %copy-start.32 = (pred[256,256]{0,1:T(8,128)(4,1)}, pred[256,256]{0,1:T(8,128)(4,1)S(1)}, u32[]{:S(2)}) copy-start(pred[256,256]{0,1:T(8,128)(4,1)S(1)} %get-tuple-element.65) | copy-start | bytes 196612
  22.1 20.7 %collective-permute-start = (bf16[2,256,256]{2,1,0:T(8,128)(2,1)S(1)}, bf16[2,256,256]{2,1,0:T(8,128)(2,1)S(1)}, u32[]{:S(2)}, u32[]{:S(2)}) collective-permute-start(bf16[2,256,256]{2,1,0:T(8,128)(2,1)S(1)} %bitcast.375), channel_id=1, source_target_pairs={{0,8},{4,12},{8,16},{12,20},{16,24},{20,28},{24,32},{28,36},{32,40... | collective-permute-start | bytes 786440 | tf_op jit(solution)/shard_map/ppermute | solution.py:19
  25.8 18.8 %collective-permute-start.1 = (bf16[2,256,256]{2,1,0:T(8,128)(2,1)S(1)}, bf16[2,256,256]{2,1,0:T(8,128)(2,1)S(1)}, u32[]{:S(2)}, u32[]{:S(2)}) collective-permute-start(bf16[2,256,256]{2,1,0:T(8,128)(2,1)S(1)} %bitcast.377), channel_id=1, source_target_pairs={{0,4},{4,8},{8,12},{12,16},{16,20},{20,24},{24,28},{28,32},{32,36}... | collective-permute-start | bytes 786440 | tf_op jit(solution)/shard_map/ppermute | solution.py:19
  29.3 34.7 %all-to-all-start.1 = ((bf16[64,4,2,512]{3,2,0,1:T(2,128)(2,1)}), bf16[64,4,2,512]{3,2,0,1:T(2,128)(2,1)S(1)}, u32[]{:S(2)}, u32[]{:S(2)}) async-start(bf16[64,4,2,512]{3,2,0,1:T(2,128)(2,1)} %copy.294), calls=%async_computation.1 | async-start | bytes 1048576 | tf_op jit(solution)/shard_map/all_to_all | solution.py:41
  32.8 17.5 %collective-permute-start.3 = (bf16[2,256,256]{2,1,0:T(8,128)(2,1)S(1)}, bf16[2,256,256]{2,1,0:T(8,128)(2,1)S(1)}, u32[]{:S(2)}, u32[]{:S(2)}) collective-permute-start(bf16[2,256,256]{2,1,0:T(8,128)(2,1)S(1)} %bitcast.373), channel_id=1, source_target_pairs={{0,4},{4,8},{8,12},{12,16},{16,20},{20,24},{24,28},{28,32},{32,36}... | collective-permute-start | bytes 786440 | tf_op jit(solution)/shard_map/ppermute | solution.py:19
  36.3 25.4 %collective-permute-start.2 = (bf16[2,256,256]{2,1,0:T(8,128)(2,1)S(1)}, bf16[2,256,256]{2,1,0:T(8,128)(2,1)S(1)}, u32[]{:S(2)}, u32[]{:S(2)}) collective-permute-start(bf16[2,256,256]{2,1,0:T(8,128)(2,1)S(1)} %bitcast.374), channel_id=1, source_target_pairs={{0,8},{4,12},{8,16},{12,20},{16,24},{20,28},{24,32},{28,36},{32,40... | collective-permute-start | bytes 786440 | tf_op jit(solution)/shard_map/ppermute | solution.py:19
  41.2 26.8 %copy-start.15 = (bf16[1,256,256]{1,2,0:T(8,128)(2,1)}, bf16[1,256,256]{1,2,0:T(8,128)(2,1)S(1)}, u32[]{:S(2)}) copy-start(bf16[1,256,256]{1,2,0:T(8,128)(2,1)S(1)} %copy.299) | copy-start | bytes 393220
  45.4 23.9 %copy-start.19 = (bf16[1,256,256]{1,2,0:T(8,128)(2,1)}, bf16[1,256,256]{1,2,0:T(8,128)(2,1)S(1)}, u32[]{:S(2)}) copy-start(bf16[1,256,256]{1,2,0:T(8,128)(2,1)S(1)} %copy.302) | copy-start | bytes 393220
  64.0 16.1 %all-to-all-start.4 = ((bf16[64,4,2,512]{3,2,0,1:T(2,128)(2,1)}), bf16[64,4,2,512]{3,2,0,1:T(2,128)(2,1)S(1)}, u32[]{:S(2)}, u32[]{:S(2)}) async-start(bf16[64,4,2,512]{3,2,0,1:T(2,128)(2,1)} %copy.325), calls=%async_computation.4 | async-start | bytes 1048576 | tf_op jit(solution)/shard_map/all_to_all | solution.py:41
  70.2 6.9 %copy-start = (f32[2,2,256,256]{2,3,1,0:T(8,128)}, f32[2,2,256,256]{2,3,1,0:T(8,128)S(1)}, u32[]{:S(2)}) copy-start(f32[2,2,256,256]{2,3,1,0:T(8,128)S(1)} %get-tuple-element.80) | copy-start | bytes 3145732
  70.2 6.3 %copy-start.42 = (f32[2,2,256]{2,1,0:T(2,128)}, f32[2,2,256]{2,1,0:T(2,128)S(1)}, u32[]{:S(2)}) copy-start(f32[2,2,256]{2,1,0:T(2,128)S(1)} %get-tuple-element.17) | copy-start | bytes 12292
  107.3 80.8 %collective-permute-start.4 = (bf16[2,256,256]{2,0,1:T(2,128)(2,1)}, bf16[2,256,256]{2,0,1:T(2,128)(2,1)}, u32[]{:S(2)}, u32[]{:S(2)}) collective-permute-start(bf16[2,256,256]{2,0,1:T(2,128)(2,1)} %pad_maximum_fusion.8), channel_id=1, source_target_pairs={{4,0},{8,4},{12,8},{16,12},{20,16},{24,20},{28,24},{32,28},{36,32}... | collective-permute-start | bytes 786440 | tf_op jit(solution)/shard_map/ppermute | solution.py:19
  116.0 72.1 %collective-permute-start.5 = (bf16[2,256,256]{2,0,1:T(2,128)(2,1)}, bf16[2,256,256]{2,0,1:T(2,128)(2,1)}, u32[]{:S(2)}, u32[]{:S(2)}) collective-permute-start(bf16[2,256,256]{2,0,1:T(2,128)(2,1)} %pad_maximum_fusion.9), channel_id=1, source_target_pairs={{8,0},{12,4},{16,8},{20,12},{24,16},{28,20},{32,24},{36,28},{40,32... | collective-permute-start | bytes 786440 | tf_op jit(solution)/shard_map/ppermute | solution.py:19
  130.1 67.3 %collective-permute-start.6 = (bf16[2,256,256]{2,0,1:T(2,128)(2,1)}, bf16[2,256,256]{2,0,1:T(2,128)(2,1)}, u32[]{:S(2)}, u32[]{:S(2)}) collective-permute-start(bf16[2,256,256]{2,0,1:T(2,128)(2,1)} %pad_maximum_fusion.10), channel_id=1, source_target_pairs={{4,0},{8,4},{12,8},{16,12},{20,16},{24,20},{28,24},{32,28},{36,32}... | collective-permute-start | bytes 786440 | tf_op jit(solution)/shard_map/ppermute | solution.py:19
  136.5 28.3 %copy-start.14 = (f32[2,128,2,256]{3,1,2,0:T(8,128)S(1)}, f32[2,128,2,256]{3,1,2,0:T(8,128)}, u32[]{:S(2)}) copy-start(f32[2,128,2,256]{3,1,2,0:T(8,128)} %fusion.92) | copy-start | bytes 1572868
  136.5 28.3 %copy-start.24 = (bf16[1,256,256]{1,2,0:T(8,128)(2,1)S(1)}, bf16[1,256,256]{1,2,0:T(8,128)(2,1)}, u32[]{:S(2)}) copy-start(bf16[1,256,256]{1,2,0:T(8,128)(2,1)} %copy.293) | copy-start | bytes 393220
  138.9 58.6 %collective-permute-start.7 = (bf16[2,256,256]{2,0,1:T(2,128)(2,1)}, bf16[2,256,256]{2,0,1:T(2,128)(2,1)}, u32[]{:S(2)}, u32[]{:S(2)}) collective-permute-start(bf16[2,256,256]{2,0,1:T(2,128)(2,1)} %pad_maximum_fusion.11), channel_id=1, source_target_pairs={{8,0},{12,4},{16,8},{20,12},{24,16},{28,20},{32,24},{36,28},{40,32... | collective-permute-start | bytes 786440 | tf_op jit(solution)/shard_map/ppermute | solution.py:19
  166.4 17.8 %all-to-all-start.2 = ((bf16[4,64,1,512]{3,1,2,0:T(8,128)(2,1)}), bf16[4,64,1,512]{3,1,2,0:T(8,128)(2,1)S(1)}, u32[]{:S(2)}, u32[]{:S(2)}) async-start(bf16[4,64,1,512]{3,1,2,0:T(8,128)(2,1)} %pad_maximum_fusion.5), calls=%async_computation.2 | async-start | bytes 524288 | tf_op jit(solution)/shard_map/all_to_all | solution.py:121
  172.6 14.9 %copy-start.5 = (bf16[256,1,1,512]{0,3,2,1:T(8,128)(2,1)S(1)}, bf16[256,1,1,512]{0,3,2,1:T(8,128)(2,1)}, u32[]{:S(2)}) copy-start(bf16[256,1,1,512]{0,3,2,1:T(8,128)(2,1)} %copy.337) | copy-start | bytes 786436
  184.1 9.4 %all-to-all-start.5 = ((bf16[4,64,1,512]{3,1,2,0:T(8,128)(2,1)}), bf16[4,64,1,512]{3,1,2,0:T(8,128)(2,1)S(1)}, u32[]{:S(2)}, u32[]{:S(2)}) async-start(bf16[4,64,1,512]{3,1,2,0:T(8,128)(2,1)} %pad_maximum_fusion.7), calls=%async_computation.5 | async-start | bytes 524288 | tf_op jit(solution)/shard_map/all_to_all | solution.py:121
  193.5 9.4 %all-to-all-start.6 = ((bf16[256,1,2,256]{3,2,1,0:T(2,128)(2,1)}), bf16[256,1,2,256]{3,2,1,0:T(2,128)(2,1)S(1)}, u32[]{:S(2)}, u32[]{:S(2)}) async-start(bf16[256,1,2,256]{3,2,1,0:T(2,128)(2,1)} %fusion.69), calls=%async_computation.6 | async-start | bytes 524288 | tf_op jit(solution)/shard_map/all_to_all | solution.py:130
  202.9 9.4 %all-to-all-start.7 = ((bf16[256,1,2,256]{3,2,1,0:T(2,128)(2,1)}), bf16[256,1,2,256]{3,2,1,0:T(2,128)(2,1)S(1)}, u32[]{:S(2)}, u32[]{:S(2)}) async-start(bf16[256,1,2,256]{3,2,1,0:T(2,128)(2,1)} %fusion.68), calls=%async_computation.7 | async-start | bytes 524288 | tf_op jit(solution)/shard_map/all_to_all | solution.py:130
  (44 other events, 72.7 us)
